TPU v7x, 32 devices: a whole 2x2x4 slice. The times are simulated.
32 devices in a mesh: row: 8 (over z, y), col: 4 (over x, core).
Axes of the slice: x: 2, y: 2, z: 4, core: 2. Of those that a mesh axis runs over, the one named last changes fastest.
Arguments:
- gram: float32 [16384, 16384], P('row', 'col'), may hold values from -1 to 17, as said below
Outputs:
- factored: float32 [16384, 16384], P('row', 'col')
Inputs may be any that keep to these rules, and one draw needn't show every extreme that they name: gram holds a symmetric positive definite matrix in the block-cyclic order of the steps.
All inputs are finite; a program needn't handle non-finite values.
Results may differ from a plain program's by a relative error of at most 0.0001.
Values sent between devices are 32-bit elements; how exact they have to be, the bound alone decides.
No kernel may reach another device: no remote copies, remote signals or barrier semaphores. Data moves between devices by JAX's collectives and lax.ppermute only.
A program may use at most 192 MiB of HBM per device.

v0:
```python
import jax
import jax.numpy as jnp
from jax import lax
from jax.sharding import PartitionSpec as P

NB = 512
STEPS = 2


def broadcast(value, axis, source):
    kept = jnp.where(lax.axis_index(axis) == source, value, 0).astype(value.dtype)
    return lax.psum(kept, axis)


def from_partner(block, axis, apart):
    count = lax.axis_size(axis)
    route = []
    for low in range(count):
        high = low | 1 << apart
        if high != low and high < count:
            route += [(low, high), (high, low)]
    return lax.ppermute(block, axis, route)


def global_index(count, block, grid, position):
    ladder = jnp.arange(count, dtype=jnp.int32)
    return (ladder // block * grid + position) * block + ladder % block


def times_transposed(left, right):
    return lax.dot_general(
        left,
        right,
        (((1,), (1,)), ((), ())),
        precision=lax.Precision.HIGHEST,
        preferred_element_type=jnp.float32,
    )


def local(gram):
    grid_rows = lax.axis_size("row")
    grid_cols = lax.axis_size("col")
    row_id = lax.axis_index("row")
    col_id = lax.axis_index("col")
    rblock = NB * grid_cols // grid_rows
    per_class = grid_rows // grid_cols
    local_rows = gram.shape[0]
    local_cols = gram.shape[1]
    blocks = local_rows // rblock
    grows = global_index(local_rows, rblock, grid_rows, row_id)
    gcols = global_index(local_cols, NB, grid_cols, col_id)
    member = row_id % per_class
    row_class = row_id // per_class
    identity = jnp.eye(NB, dtype=jnp.float32)

    def factor_panel(matrix, panel_index):
        owner_col = panel_index % grid_cols
        local_block = panel_index // grid_cols
        end_row = panel_index * NB + NB
        column = matrix[:, local_block * NB : (local_block + 1) * NB]
        square = column[local_block * rblock : (local_block + 1) * rblock]
        is_owner = col_id == owner_col
        in_class = row_class == owner_col
        select = (jnp.arange(per_class, dtype=jnp.int32) == member).astype(jnp.float32)
        weight = jnp.where(is_owner & in_class, 1.0, 0.0).astype(jnp.float32)
        placed = (select[:, None, None] * square[None]).reshape(NB, NB) * weight
        diagonal = lax.psum(placed, "row")
        diagonal = jnp.where(is_owner, diagonal, identity)
        low_factor = jnp.linalg.cholesky(diagonal)
        inverse = jax.scipy.linalg.solve_triangular(low_factor, identity, lower=True)
        solved = times_transposed(column, inverse)
        trailing = jnp.where((grows >= end_row)[:, None], solved, 0.0)
        rows_diag = lax.dynamic_slice_in_dim(low_factor, member * rblock, rblock, 0)
        previous = trailing[local_block * rblock : (local_block + 1) * rblock]
        patched = jnp.where(in_class, rows_diag, previous)
        factored = trailing.at[local_block * rblock : (local_block + 1) * rblock].set(patched)
        new_column = jnp.where(is_owner, factored, column)
        matrix = matrix.at[:, local_block * NB : (local_block + 1) * NB].set(new_column)
        return (matrix, trailing)

    matrix = gram
    for panel_index in range(STEPS):
        matrix, trailing = factor_panel(matrix, panel_index)
        spread_owner_col = panel_index % grid_cols
        spread_rows_all = broadcast(trailing, "col", spread_owner_col)
        pieces = spread_rows_all.reshape(grid_cols, blocks // grid_cols * rblock, NB)
        shift_bits = per_class.bit_length() - 1
        for bit_level in reversed(range(grid_cols.bit_length() - 1)):
            halfway = pieces.shape[0] // 2
            own_bit = row_class >> bit_level & 1
            wanted = col_id >> bit_level & 1
            upper = own_bit == 1
            retained = jnp.where(upper, pieces[halfway:], pieces[:halfway])
            outgoing = jnp.where(upper, pieces[:halfway], pieces[halfway:])
            received = from_partner(outgoing, "row", shift_bits + bit_level)
            pieces = jnp.where(own_bit == wanted, retained, received)
        gathered = lax.all_gather(pieces[0], "row", axis=0, tiled=True)
        spread_columns = gathered.reshape(grid_cols, per_class, blocks // grid_cols, rblock, NB)
        spread_columns = jnp.transpose(spread_columns, (0, 2, 1, 3, 4)).reshape(local_cols, NB)
        first_row = panel_index * NB
        apply_end_row = first_row + NB
        current = matrix
        updated = current - times_transposed(spread_rows_all, spread_columns)
        panel_rows = (grows >= first_row) & (grows < apply_end_row)
        beyond = gcols >= apply_end_row
        updated = jnp.where(panel_rows[:, None] & beyond[None, :], 0.0, updated)
        matrix = matrix.at[:, 0:local_cols].set(updated)
    matrix, trailing = factor_panel(matrix, STEPS)
    return matrix


def solution(mesh):
    placed = (P("row", "col"),)
    return jax.shard_map(
        local, mesh=mesh, in_specs=placed, out_specs=P("row", "col"), check_vma=False
    )
```

profile of v0, /device:TPU:0, one launch (start us, length us, event | category | flops | bytes accessed | tf_op | source)
XLA Modules:
  0.0 1543.9 jit_solution(489001765417519902)
XLA Ops:
  6.5 23.0 %copy.106 = f32[2048,4096]{1,0:T(8,128)} copy(f32[2048,4096]{1,0:T(8,128)} %param.24) | data formatting | bytes 67108864
  32.8 81.1 %all-reduce.7.cloned.1.call-done = f32[512,512]{0,1:T(8,128)} async-done(((f32[512,512]{0,1:T(8,128)}), f32[512,512]{0,1:T(8,128)}) %all-reduce.7.cloned.1.call-update) | async-done | bytes 1048592 | tf_op jit(solution)/shard_map/psum | solution.py:67
  113.9 1.4 convert_select_fusion.2
  116.7 1.5 fusion.40
  118.1 11.7 cholesky.374
  130.0 9.8 custom-call.31
  140.5 11.7 cholesky.393
  152.3 10.0 custom-call.32
  162.9 11.7 cholesky.414
  174.6 9.8 custom-call.33
  185.1 11.7 cholesky.431
  203.0 8.4 while.16
  203.7 1.4 bitcast_dynamic-update-slice_fusion.6
  211.4 39.3 %custom-call.34 = f32[4,128,128]{1,2,0:T(8,128)S(1)} custom-call(f32[4,128,128]{2,1,0:T(8,128)S(1)} %get-tuple-element.139), custom_call_target="InvertDiagBlocksLowerTriangular" | custom-call | tf_op jit(solution)/shard_map/jit(_solve_triangular)/triangular_solve | solution.py:70
  253.6 1.5 convolution_subtract_fusion.8
  255.5 10.6 broadcast_select_fusion.1
  266.2 84.3 %all-reduce.9.cloned.1.call-done = f32[2048,512]{1,0:T(8,128)} async-done(((f32[2048,512]{1,0:T(8,128)}), f32[2048,512]{1,0:T(8,128)}) %all-reduce.9.cloned.1.call-update) | async-done | bytes 4194320 | tf_op jit(solution)/shard_map/psum | solution.py:12
  350.5 4.8 slice_select_fusion.2
  355.3 2.4 collective-permute-start
  357.7 90.7 %collective-permute-done = f32[2,512,512]{2,1,0:T(8,128)S(1)} collective-permute-done((f32[2,512,512]{2,1,0:T(8,128)}, f32[2,512,512]{2,1,0:T(8,128)S(1)}, u32[]{:S(2)}, u32[]{:S(2)}) %collective-permute-start) | collective-permute-done | bytes 2097184 | tf_op jit(solution)/shard_map/ppermute | solution.py:22
  449.7 2.1 broadcast_select_fusion.3
  453.6 23.9 %collective-permute-done.1 = f32[1,512,512]{2,1,0:T(8,128)} collective-permute-done((f32[1,512,512]{2,1,0:T(8,128)}, f32[1,512,512]{2,1,0:T(8,128)}, u32[]{:S(2)}, u32[]{:S(2)}) %collective-permute-start.1) | collective-permute-done | bytes 1048608 | tf_op jit(solution)/shard_map/ppermute | solution.py:22
  480.1 2.1 fusion.63
  482.2 7.1 fusion
  489.3 116.8 %all-gather.5.cloned.1.call-done = f32[1,4096,512]{2,1,0:T(8,128)} async-done(((f32[1,512,512]{2,1,0:T(8,128)}), f32[1,4096,512]{2,1,0:T(8,128)}) %all-gather.5.cloned.1.call-update) | async-done | bytes 8388624 | tf_op jit(solution)/shard_map/all_gather | solution.py:97
  606.1 4.6 copy.22
  610.7 60.7 %subtract_select_fusion.1 = f32[2048,4096]{1,0:T(8,128)} fusion(f32[2048,4096]{1,0:T(8,128)} %fusion, pred[4096]{0:T(1024)(128)(4,1)S(1)} %broadcast_compare_fusion.1, pred[2048]{0:T(1024)(128)(4,1)S(1)} %get-tuple-element.222, f32[2048,512]{1,0:T(8,128)S(1)} %copy-done, f32[4096,512]{1,0:T(8,128)S(1)} %bitcast.177), kind=kOutput, calls=%fused_computation.7 | convolution fusion | flops 51564773376 | bytes 79697920 | tf_op jit(solution)/shard_map/dot_general | solution.py:31
  674.6 76.4 %all-reduce.11.cloned.1.call-done = f32[512,512]{0,1:T(8,128)} async-done(((f32[512,512]{0,1:T(8,128)}), f32[512,512]{0,1:T(8,128)}) %all-reduce.11.cloned.1.call-update) | async-done | bytes 1048592 | tf_op jit(solution)/shard_map/psum | solution.py:67
  752.5 1.5 fusion.39
  754.0 11.7 cholesky.446
  765.9 9.8 custom-call.35
  776.4 11.7 cholesky.465
  788.1 10.0 custom-call.36
  798.8 11.7 cholesky.486
  810.6 9.8 custom-call.37
  821.0 11.7 cholesky.503
  839.8 8.4 while.17
  848.2 39.3 %custom-call.38 = f32[4,128,128]{1,2,0:T(8,128)S(1)} custom-call(f32[4,128,128]{2,1,0:T(8,128)S(1)} %get-tuple-element.140), custom_call_target="InvertDiagBlocksLowerTriangular" | custom-call | tf_op jit(solution)/shard_map/jit(_solve_triangular)/triangular_solve | solution.py:70
  890.4 1.5 convolution_subtract_fusion.7
  892.3 10.6 broadcast_select_fusion
  903.1 85.0 %all-reduce.13.cloned.1.call-done = f32[2048,512]{1,0:T(8,128)} async-done(((f32[2048,512]{1,0:T(8,128)}), f32[2048,512]{1,0:T(8,128)}) %all-reduce.13.cloned.1.call-update) | async-done | bytes 4194320 | tf_op jit(solution)/shard_map/psum | solution.py:12
  988.1 2.8 slice_select_fusion
  990.9 2.5 collective-permute-start.2
  993.4 90.5 %collective-permute-done.2 = f32[2,512,512]{2,1,0:T(8,128)S(1)} collective-permute-done((f32[2,512,512]{2,1,0:T(8,128)S(1)}, f32[2,512,512]{2,1,0:T(8,128)S(1)}, u32[]{:S(2)}, u32[]{:S(2)}) %collective-permute-start.2) | collective-permute-done | bytes 2097184 | tf_op jit(solution)/shard_map/ppermute | solution.py:22
  1085.1 23.7 %collective-permute-done.3 = f32[1,512,512]{2,1,0:T(8,128)S(1)} collective-permute-done((f32[1,512,512]{2,1,0:T(8,128)S(1)}, f32[1,512,512]{2,1,0:T(8,128)S(1)}, u32[]{:S(2)}, u32[]{:S(2)}) %collective-permute-start.3) | collective-permute-done | bytes 1048608 | tf_op jit(solution)/shard_map/ppermute | solution.py:22
  1110.3 2.0 fusion.62
  1112.3 5.8 fusion.1
  1118.1 118.1 %all-gather.7.cloned.1.call-done = f32[1,4096,512]{2,1,0:T(8,128)} async-done(((f32[1,512,512]{2,1,0:T(8,128)}), f32[1,4096,512]{2,1,0:T(8,128)}) %all-gather.7.cloned.1.call-update) | async-done | bytes 8388624 | tf_op jit(solution)/shard_map/all_gather | solution.py:97
  1236.2 4.6 copy.28
  1240.8 60.9 %subtract_select_fusion = f32[2048,4096]{1,0:T(8,128)} fusion(f32[2048,4096]{1,0:T(8,128)} %fusion.1, pred[4096]{0:T(1024)(128)(4,1)S(1)} %broadcast_compare_fusion, pred[2048]{0:T(1024)(128)(4,1)S(1)} %compare_and_fusion.1, f32[2048,512]{1,0:T(8,128)S(1)} %copy-done.1, f32[4096,512]{1,0:T(8,128)S(1)} %bitcast.178), kind=kOutput, calls=%fused_computation.6 | convolution fusion | flops 51564773376 | bytes 79697920 | tf_op jit(solution)/shard_map/dot_general | solution.py:31
  1304.6 76.6 %all-reduce.15.cloned.1.call-done = f32[512,512]{0,1:T(8,128)} async-done(((f32[512,512]{0,1:T(8,128)}), f32[512,512]{0,1:T(8,128)}) %all-reduce.15.cloned.1.call-update) | async-done | bytes 1048592 | tf_op jit(solution)/shard_map/psum | solution.py:67
  1382.8 1.5 fusion.38
  1384.3 11.7 cholesky.518
  1396.1 9.8 custom-call.39
  1406.6 11.7 cholesky.537
  1418.4 10.2 custom-call.40
  1429.3 11.7 cholesky.558
  1441.0 9.8 custom-call.41
  1451.4 11.9 cholesky.575
  1469.8 8.1 while.18
  1478.0 39.3 %custom-call.42 = f32[4,128,128]{1,2,0:T(8,128)S(1)} custom-call(f32[4,128,128]{2,1,0:T(8,128)S(1)} %get-tuple-element.141), custom_call_target="InvertDiagBlocksLowerTriangular" | custom-call | tf_op jit(solution)/shard_map/jit(_solve_triangular)/triangular_solve | solution.py:70
  1520.2 1.5 convolution_subtract_fusion.6
  1522.1 8.7 fusion.14
  1531.0 5.8 fusion.2
  (183 shorter events, 73.8 us)
Async XLA Ops:
  6.5 107.3 %all-reduce.7.cloned.1.call-start = ((), (), s32[]{:S(2)}) async-start(), calls=%async_computation | async-start | bytes 2097152 | tf_op jit(solution)/shard_map/psum | solution.py:67
  32.6 317.9 %all-reduce.9.cloned.1.call-start = ((), (), s32[]{:S(2)}) async-start(), calls=%async_computation.1 | async-start | bytes 8388608 | tf_op jit(solution)/shard_map/psum | solution.py:12
  113.9 2.8 copy-start.2
  266.2 340.0 %all-gather.5.cloned.1.call-start = ((), (), s32[]{:S(2)}) async-start(), calls=%async_computation.5 | async-start | bytes 9437184 | tf_op jit(solution)/shard_map/all_gather | solution.py:97
  355.3 93.1 %collective-permute-start = (f32[2,512,512]{2,1,0:T(8,128)}, f32[2,512,512]{2,1,0:T(8,128)S(1)}, u32[]{:S(2)}, u32[]{:S(2)}) collective-permute-start(f32[2,512,512]{2,1,0:T(8,128)} %bitcast.13), channel_id=1, source_target_pairs={{0,16},{16,0},{4,20},{20,4},{8,24},{24,8},{12,28},{28,12},{1,17},{... | collective-permute-start | bytes 6291464 | tf_op jit(solution)/shard_map/ppermute | solution.py:22
  448.4 1.3 copy-start.7
  453.0 24.5 %collective-permute-start.1 = (f32[1,512,512]{2,1,0:T(8,128)}, f32[1,512,512]{2,1,0:T(8,128)}, u32[]{:S(2)}, u32[]{:S(2)}) collective-permute-start(f32[1,512,512]{2,1,0:T(8,128)} %slice_select_fusion.5), channel_id=1, source_target_pairs={{0,8},{8,0},{4,12},{12,4},{16,24},{24,16},{20,28},{28,20},{1,9},{9... | collective-permute-start | bytes 3145736 | tf_op jit(solution)/shard_map/ppermute | solution.py:22
  478.9 272.1 %all-reduce.11.cloned.1.call-start = ((), (), s32[]{:S(2)}) async-start(), calls=%async_computation.2 | async-start | bytes 2097152 | tf_op jit(solution)/shard_map/psum | solution.py:67
  606.1 4.6 copy-start
  674.4 313.7 %all-reduce.13.cloned.1.call-start = ((), (), s32[]{:S(2)}) async-start(), calls=%async_computation.3 | async-start | bytes 8388608 | tf_op jit(solution)/shard_map/psum | solution.py:12
  751.0 1.5 copy-start.3
  902.9 333.3 %all-gather.7.cloned.1.call-start = ((), (), s32[]{:S(2)}) async-start(), calls=%async_computation.6 | async-start | bytes 9437184 | tf_op jit(solution)/shard_map/all_gather | solution.py:97
  990.9 93.0 %collective-permute-start.2 = (f32[2,512,512]{2,1,0:T(8,128)S(1)}, f32[2,512,512]{2,1,0:T(8,128)S(1)}, u32[]{:S(2)}, u32[]{:S(2)}) collective-permute-start(f32[2,512,512]{2,1,0:T(8,128)S(1)} %bitcast.189), channel_id=1, source_target_pairs={{0,16},{16,0},{4,20},{20,4},{8,24},{24,8},{12,28},{28,12},{1,17},{... | collective-permute-start | bytes 6291464 | tf_op jit(solution)/shard_map/ppermute | solution.py:22
  1084.3 26.0 %copy-start.5 = (f32[512,512]{1,0:T(8,128)S(1)}, f32[512,512]{1,0:T(8,128)}, u32[]{:S(2)}) copy-start(f32[512,512]{1,0:T(8,128)} %get-tuple-element.169) | copy-start | bytes 3145732
  1084.6 24.2 %collective-permute-start.3 = (f32[1,512,512]{2,1,0:T(8,128)S(1)}, f32[1,512,512]{2,1,0:T(8,128)S(1)}, u32[]{:S(2)}, u32[]{:S(2)}) collective-permute-start(f32[1,512,512]{2,1,0:T(8,128)S(1)} %slice_select_fusion.4), channel_id=1, source_target_pairs={{0,8},{8,0},{4,12},{12,4},{16,24},{24,16},{20,28},{28,20},{1,9},{9... | collective-permute-start | bytes 3145736 | tf_op jit(solution)/shard_map/ppermute | solution.py:22
  1110.2 271.1 %all-reduce.15.cloned.1.call-start = ((), (), s32[]{:S(2)}) async-start(), calls=%async_computation.4 | async-start | bytes 2097152 | tf_op jit(solution)/shard_map/psum | solution.py:67
  1236.2 4.6 copy-start.1
  1381.3 1.5 copy-start.4
  1522.1 8.7 copy-start.6
Sparse Core Ops, SparseCore 0:
  32.7 81.0 all-reduce.6
  266.3 84.1 all-reduce.8
  479.1 127.0 all-gather.4
  674.5 76.4 all-reduce.10
  903.0 85.0 all-reduce.12
  1110.3 125.8 all-gather.6
  1304.7 76.4 all-reduce.14
where the time goes:
time: 1550 us; the launch traced here: 1540 us
  waiting for transfers between devices  867 us (56%)
  other arithmetic  408 us (26%)
  matrix products  171 us (11%)
  local copies, waits for them, and re-layouts  67.9 us (4%)
  between operations  22.3 us (1%)
    another operation x44, other arithmetic, factor_panel(): low_factor = jnp.linalg.cholesky(diagonal)  238 us
    all_gather x2, waiting for transfers between devices, local(): gathered = lax.all_gather(pieces[0], 'row', axis=0, tiled=True)  235 us
    psum x3, waiting for transfers between devices, factor_panel(): diagonal = lax.psum(placed, 'row')  234 us
    ppermute x4, waiting for transfers between devices, from_partner(): return lax.ppermute(block, axis, route)  229 us
    psum x2, waiting for transfers between devices, broadcast(): return lax.psum(kept, axis)  169 us
    dot_general x5, matrix products, times_transposed(): lax.dot_general(left, right, (((1,), (1,)), ((), ())), precision=lax.Prec...  152 us
    another operation x7, other arithmetic, factor_panel(): jax.scipy.linalg.solve_triangular(low_factor, identity, lower=True)  122 us
  transfers between devices with their start and end apart: 11, of which 11 were waited for; matrix products, arithmetic and copies ran while one was open for 1% of the time, Pallas kernels for 0%

commit v1 on v0

--- a/solution.py
+++ b/solution.py
@@ -5,6 +5,18 @@
 
 NB = 512
 STEPS = 2
+
+
+def gather_by_bits(x, axis, dim):
+    ways, here = (lax.axis_size(axis), lax.axis_index(axis))
+    grown, reach = (x, 1)
+    while reach < ways:
+        theirs = lax.ppermute(grown, axis, [(d, d ^ reach) for d in range(ways)])
+        mine_first = jnp.concatenate([grown, theirs], axis=dim)
+        theirs_first = jnp.concatenate([theirs, grown], axis=dim)
+        grown = jnp.where(here & reach == 0, mine_first, theirs_first)
+        reach = 2 * reach
+    return grown
 
 
 def broadcast(value, axis, source):
@@ -94,7 +106,7 @@
             outgoing = jnp.where(upper, pieces[:halfway], pieces[halfway:])
             received = from_partner(outgoing, "row", shift_bits + bit_level)
             pieces = jnp.where(own_bit == wanted, retained, received)
-        gathered = lax.all_gather(pieces[0], "row", axis=0, tiled=True)
+        gathered = gather_by_bits(pieces[0], "row", 0)
         spread_columns = gathered.reshape(grid_cols, per_class, blocks // grid_cols, rblock, NB)
         spread_columns = jnp.transpose(spread_columns, (0, 2, 1, 3, 4)).reshape(local_cols, NB)
         first_row = panel_index * NB

time: 1550 us -> 1840 us (1.19)
  waiting for transfers between devices: 867 us -> 1110 us
  other arithmetic: 408 us -> 441 us
    ppermute x0 -> x6, waiting for transfers between devices: none -> 474 us  [gather_by_bits(): theirs = lax.ppermute(grown, axis, [(d, d ^ reach) for d in range(ways)])]
    all_gather x2 -> x0, waiting for transfers between devices: 235 us -> none  [local(): gathered = lax.all_gather(pieces[0], 'row', axis=0, tiled=True)]
    select_n x0 -> x6, other arithmetic: none -> 24 us  [gather_by_bits(): grown = jnp.where(here & reach == 0, mine_first, theirs_first)]
  transfers between devices with their start and end apart: 11 -> 15, of which waited for: 11 -> 15; matrix products, arithmetic and copies ran while one was open for 1% -> 1% of each run, Pallas kernels for 0% -> 0%
where the time goes in v1:
time: 1840 us; the launch traced here: 1830 us
  waiting for transfers between devices  1110 us (60%)
  other arithmetic  441 us (24%)
  matrix products  172 us (9%)
  local copies, waits for them, and re-layouts  62.6 us (3%)
  starting transfers between devices  22.7 us (1%)
  between operations  22 us (1%)
    ppermute x6, waiting for transfers between devices, gather_by_bits(): theirs = lax.ppermute(grown, axis, [(d, d ^ reach) for d in range(ways)])  474 us
    another operation x44, other arithmetic, factor_panel(): low_factor = jnp.linalg.cholesky(diagonal)  248 us
    psum x3, waiting for transfers between devices, factor_panel(): diagonal = lax.psum(placed, 'row')  238 us
    ppermute x4, waiting for transfers between devices, from_partner(): return lax.ppermute(block, axis, route)  229 us
    psum x2, waiting for transfers between devices, broadcast(): return lax.psum(kept, axis)  169 us
    dot_general x5, matrix products, times_transposed(): lax.dot_general(left, right, (((1,), (1,)), ((), ())), precision=lax.Prec...  152 us
    another operation x7, other arithmetic, factor_panel(): jax.scipy.linalg.solve_triangular(low_factor, identity, lower=True)  122 us
  transfers between devices with their start and end apart: 15, of which 15 were waited for; matrix products, arithmetic and copies ran while one was open for 1% of the time, Pallas kernels for 0%

profile of v1, /device:TPU:0, one launch (start us, length us, event | category | flops | bytes accessed | tf_op | source)
XLA Modules:
  0.0 1829.9 jit_solution(8755437384180130347)
XLA Ops:
  6.5 23.0 %copy.106 = f32[2048,4096]{1,0:T(8,128)} copy(f32[2048,4096]{1,0:T(8,128)} %param.24) | data formatting | bytes 67108864
  32.8 81.1 %all-reduce.7.cloned.1.call-done = f32[512,512]{0,1:T(8,128)} async-done(((f32[512,512]{0,1:T(8,128)}), f32[512,512]{0,1:T(8,128)}) %all-reduce.7.cloned.1.call-update) | async-done | bytes 1048592 | tf_op jit(solution)/shard_map/psum | solution.py:79
  118.1 11.7 cholesky.374
  130.0 9.8 custom-call.31
  140.5 11.7 cholesky.393
  152.3 10.0 custom-call.32
  163.0 11.7 cholesky.414
  174.7 9.8 custom-call.33
  185.1 11.7 cholesky.431
  196.9 10.6 compare_reduce_fusion.9
  212.7 8.1 while.16
  220.8 39.3 %custom-call.34 = f32[4,128,128]{1,2,0:T(8,128)S(1)} custom-call(f32[4,128,128]{2,1,0:T(8,128)S(1)} %get-tuple-element.139), custom_call_target="InvertDiagBlocksLowerTriangular" | custom-call | tf_op jit(solution)/shard_map/jit(_solve_triangular)/triangular_solve | solution.py:82
  264.9 10.6 broadcast_select_fusion.1
  275.6 84.3 %all-reduce.9.cloned.1.call-done = f32[2048,512]{1,0:T(8,128)} async-done(((f32[2048,512]{1,0:T(8,128)}), f32[2048,512]{1,0:T(8,128)}) %all-reduce.9.cloned.1.call-update) | async-done | bytes 4194320 | tf_op jit(solution)/shard_map/psum | solution.py:24
  359.9 4.9 slice_select_fusion.2
  364.8 2.4 collective-permute-start
  367.2 90.7 %collective-permute-done = f32[2,512,512]{2,1,0:T(8,128)S(1)} collective-permute-done((f32[2,512,512]{2,1,0:T(8,128)}, f32[2,512,512]{2,1,0:T(8,128)S(1)}, u32[]{:S(2)}, u32[]{:S(2)}) %collective-permute-start) | collective-permute-done | bytes 2097184 | tf_op jit(solution)/shard_map/ppermute | solution.py:34
  463.1 23.9 %collective-permute-done.1 = f32[1,512,512]{2,1,0:T(8,128)} collective-permute-done((f32[1,512,512]{2,1,0:T(8,128)}, f32[1,512,512]{2,1,0:T(8,128)}, u32[]{:S(2)}, u32[]{:S(2)}) %collective-permute-start.1) | collective-permute-done | bytes 1048608 | tf_op jit(solution)/shard_map/ppermute | solution.py:34
  489.7 23.4 %collective-permute-done.2 = f32[512,512]{1,0:T(8,128)} collective-permute-done((f32[512,512]{1,0:T(8,128)}, f32[512,512]{1,0:T(8,128)}, u32[]{:S(2)}, u32[]{:S(2)}) %collective-permute-start.2) | collective-permute-done | bytes 1048608 | tf_op jit(solution)/shard_map/ppermute | solution.py:14
  513.1 2.9 maximum_select_fusion.4
  517.3 45.0 %collective-permute-done.3 = f32[1024,512]{1,0:T(8,128)} collective-permute-done((f32[1024,512]{1,0:T(8,128)S(1)}, f32[1024,512]{1,0:T(8,128)}, u32[]{:S(2)}, u32[]{:S(2)}) %collective-permute-start.3) | collective-permute-done | bytes 2097184 | tf_op jit(solution)/shard_map/ppermute | solution.py:14
  562.3 5.2 maximum_select_fusion.2
  567.5 5.5 collective-permute-start.4
  576.2 7.2 fusion
  583.4 169.2 %collective-permute-done.4 = f32[2048,512]{1,0:T(8,128)} collective-permute-done((f32[2048,512]{1,0:T(8,128)}, f32[2048,512]{1,0:T(8,128)}, u32[]{:S(2)}, u32[]{:S(2)}) %collective-permute-start.4) | collective-permute-done | bytes 4194336 | tf_op jit(solution)/shard_map/ppermute | solution.py:14
  752.6 6.4 maximum_select_fusion
  761.2 60.7 %subtract_select_fusion.1 = f32[2048,4096]{1,0:T(8,128)} fusion(f32[2048,4096]{1,0:T(8,128)} %fusion, pred[4096]{0:T(1024)(128)(4,1)S(1)} %broadcast_compare_fusion.1, pred[2048]{0:T(1024)(128)(4,1)S(1)} %get-tuple-element.222, f32[2048,512]{1,0:T(8,128)S(1)} %copy-done, f32[4096,512]{1,0:T(8,128)S(1)} %bitcast.183), kind=kOutput, calls=%fused_computation.7 | convolution fusion | flops 51564773376 | bytes 79697920 | tf_op jit(solution)/shard_map/dot_general | solution.py:43
  825.1 78.1 %all-reduce.11.cloned.1.call-done = f32[512,512]{0,1:T(8,128)} async-done(((f32[512,512]{0,1:T(8,128)}), f32[512,512]{0,1:T(8,128)}) %all-reduce.11.cloned.1.call-update) | async-done | bytes 1048592 | tf_op jit(solution)/shard_map/psum | solution.py:79
  906.1 11.7 cholesky.446
  918.0 9.8 custom-call.35
  928.5 11.7 cholesky.465
  940.3 10.0 custom-call.36
  950.9 11.7 cholesky.486
  962.7 9.8 custom-call.37
  973.1 11.7 cholesky.503
  991.7 8.1 while.17
  999.9 39.3 %custom-call.38 = f32[4,128,128]{1,2,0:T(8,128)S(1)} custom-call(f32[4,128,128]{2,1,0:T(8,128)S(1)} %get-tuple-element.140), custom_call_target="InvertDiagBlocksLowerTriangular" | custom-call | tf_op jit(solution)/shard_map/jit(_solve_triangular)/triangular_solve | solution.py:82
  1044.0 10.6 broadcast_select_fusion
  1054.8 85.0 %all-reduce.13.cloned.1.call-done = f32[2048,512]{1,0:T(8,128)} async-done(((f32[2048,512]{1,0:T(8,128)}), f32[2048,512]{1,0:T(8,128)}) %all-reduce.13.cloned.1.call-update) | async-done | bytes 4194320 | tf_op jit(solution)/shard_map/psum | solution.py:24
  1139.8 2.8 slice_select_fusion
  1142.6 2.5 collective-permute-start.5
  1145.1 90.5 %collective-permute-done.5 = f32[2,512,512]{2,1,0:T(8,128)S(1)} collective-permute-done((f32[2,512,512]{2,1,0:T(8,128)S(1)}, f32[2,512,512]{2,1,0:T(8,128)S(1)}, u32[]{:S(2)}, u32[]{:S(2)}) %collective-permute-start.5) | collective-permute-done | bytes 2097184 | tf_op jit(solution)/shard_map/ppermute | solution.py:34
  1236.8 23.7 %collective-permute-done.6 = f32[1,512,512]{2,1,0:T(8,128)S(1)} collective-permute-done((f32[1,512,512]{2,1,0:T(8,128)S(1)}, f32[1,512,512]{2,1,0:T(8,128)S(1)}, u32[]{:S(2)}, u32[]{:S(2)}) %collective-permute-start.6) | collective-permute-done | bytes 1048608 | tf_op jit(solution)/shard_map/ppermute | solution.py:34
  1262.4 21.8 %collective-permute-done.7 = f32[512,512]{1,0:T(8,128)S(1)} collective-permute-done((f32[512,512]{1,0:T(8,128)S(1)}, f32[512,512]{1,0:T(8,128)S(1)}, u32[]{:S(2)}, u32[]{:S(2)}) %collective-permute-start.7) | collective-permute-done | bytes 1048608 | tf_op jit(solution)/shard_map/ppermute | solution.py:14
  1284.5 2.4 collective-permute-start.8
  1286.9 44.1 %collective-permute-done.8 = f32[1024,512]{1,0:T(8,128)S(1)} collective-permute-done((f32[1024,512]{1,0:T(8,128)S(1)}, f32[1024,512]{1,0:T(8,128)S(1)}, u32[]{:S(2)}, u32[]{:S(2)}) %collective-permute-start.8) | collective-permute-done | bytes 2097184 | tf_op jit(solution)/shard_map/ppermute | solution.py:14
  1331.0 2.8 maximum_select_fusion.3
  1333.8 3.9 collective-permute-start.9
  1339.7 5.9 fusion.1
  1345.6 170.8 %collective-permute-done.9 = f32[2048,512]{1,0:T(8,128)} collective-permute-done((f32[2048,512]{1,0:T(8,128)}, f32[2048,512]{1,0:T(8,128)}, u32[]{:S(2)}, u32[]{:S(2)}) %collective-permute-start.9) | collective-permute-done | bytes 4194336 | tf_op jit(solution)/shard_map/ppermute | solution.py:14
  1516.4 6.4 maximum_select_fusion.1
  1525.0 61.1 %subtract_select_fusion = f32[2048,4096]{1,0:T(8,128)} fusion(f32[2048,4096]{1,0:T(8,128)} %fusion.1, pred[4096]{0:T(1024)(128)(4,1)S(1)} %broadcast_compare_fusion, pred[2048]{0:T(1024)(128)(4,1)S(1)} %compare_and_fusion.1, f32[2048,512]{1,0:T(8,128)S(1)} %copy-done.1, f32[4096,512]{1,0:T(8,128)S(1)} %bitcast.184), kind=kOutput, calls=%fused_computation.6 | convolution fusion | flops 51564773376 | bytes 79697920 | tf_op jit(solution)/shard_map/dot_general | solution.py:43
  1589.1 78.6 %all-reduce.15.cloned.1.call-done = f32[512,512]{0,1:T(8,128)} async-done(((f32[512,512]{0,1:T(8,128)}), f32[512,512]{0,1:T(8,128)}) %all-reduce.15.cloned.1.call-update) | async-done | bytes 1048592 | tf_op jit(solution)/shard_map/psum | solution.py:79
  1670.6 11.7 cholesky.518
  1682.5 9.8 custom-call.39
  1693.0 11.7 cholesky.537
  1704.7 9.9 custom-call.40
  1715.4 11.7 cholesky.558
  1727.1 9.8 custom-call.41
  1737.5 11.9 cholesky.575
  1756.0 8.1 while.18
  1764.1 39.3 %custom-call.42 = f32[4,128,128]{1,2,0:T(8,128)S(1)} custom-call(f32[4,128,128]{2,1,0:T(8,128)S(1)} %get-tuple-element.141), custom_call_target="InvertDiagBlocksLowerTriangular" | custom-call | tf_op jit(solution)/shard_map/jit(_solve_triangular)/triangular_solve | solution.py:82
  1808.3 8.7 fusion.14
  1817.1 5.9 fusion.2
  (195 shorter events, 97.6 us)
Async XLA Ops:
  6.5 107.3 %all-reduce.7.cloned.1.call-start = ((), (), s32[]{:S(2)}) async-start(), calls=%async_computation | async-start | bytes 2097152 | tf_op jit(solution)/shard_map/psum | solution.py:79
  32.6 327.3 %all-reduce.9.cloned.1.call-start = ((), (), s32[]{:S(2)}) async-start(), calls=%async_computation.1 | async-start | bytes 8388608 | tf_op jit(solution)/shard_map/psum | solution.py:24
  113.9 2.8 copy-start.2
  275.6 627.6 %all-reduce.11.cloned.1.call-start = ((), (), s32[]{:S(2)}) async-start(), calls=%async_computation.2 | async-start | bytes 2097152 | tf_op jit(solution)/shard_map/psum | solution.py:79
  364.8 93.1 %collective-permute-start = (f32[2,512,512]{2,1,0:T(8,128)}, f32[2,512,512]{2,1,0:T(8,128)S(1)}, u32[]{:S(2)}, u32[]{:S(2)}) collective-permute-start(f32[2,512,512]{2,1,0:T(8,128)} %bitcast.13), channel_id=1, source_target_pairs={{0,16},{16,0},{4,20},{20,4},{8,24},{24,8},{12,28},{28,12},{1,17},{... | collective-permute-start | bytes 6291464 | tf_op jit(solution)/shard_map/ppermute | solution.py:34
  457.9 1.3 copy-start.7
  462.5 24.5 %collective-permute-start.1 = (f32[1,512,512]{2,1,0:T(8,128)}, f32[1,512,512]{2,1,0:T(8,128)}, u32[]{:S(2)}, u32[]{:S(2)}) collective-permute-start(f32[1,512,512]{2,1,0:T(8,128)} %slice_select_fusion.5), channel_id=1, source_target_pairs={{0,8},{8,0},{4,12},{12,4},{16,24},{24,16},{20,28},{28,20},{1,9},{9... | collective-permute-start | bytes 3145736 | tf_op jit(solution)/shard_map/ppermute | solution.py:34
  488.3 24.8 %collective-permute-start.2 = (f32[512,512]{1,0:T(8,128)}, f32[512,512]{1,0:T(8,128)}, u32[]{:S(2)}, u32[]{:S(2)}) collective-permute-start(f32[512,512]{1,0:T(8,128)} %select_bitcast_fusion.2), channel_id=1, source_target_pairs={{0,4},{4,0},{8,12},{12,8},{16,20},{20,16},{24,28},{28,24},{1,5},{5... | collective-permute-start | bytes 3145736 | tf_op jit(solution)/shard_map/ppermute | solution.py:14
  516.0 46.3 %collective-permute-start.3 = (f32[1024,512]{1,0:T(8,128)S(1)}, f32[1024,512]{1,0:T(8,128)}, u32[]{:S(2)}, u32[]{:S(2)}) collective-permute-start(f32[1024,512]{1,0:T(8,128)S(1)} %maximum_select_fusion.4), channel_id=1, source_target_pairs={{0,8},{4,12},{8,0},{12,4},{16,24},{20,28},{24,16},{28,20},{1,9},{5... | collective-permute-start | bytes 6291464 | tf_op jit(solution)/shard_map/ppermute | solution.py:14
  567.5 185.1 %collective-permute-start.4 = (f32[2048,512]{1,0:T(8,128)}, f32[2048,512]{1,0:T(8,128)}, u32[]{:S(2)}, u32[]{:S(2)}) collective-permute-start(f32[2048,512]{1,0:T(8,128)} %maximum_select_fusion.2), channel_id=1, source_target_pairs={{0,16},{4,20},{8,24},{12,28},{16,0},{20,4},{24,8},{28,12},{1,17},{... | collective-permute-start | bytes 12582920 | tf_op jit(solution)/shard_map/ppermute | solution.py:14
  759.0 2.2 copy-start
  824.9 315.0 %all-reduce.13.cloned.1.call-start = ((), (), s32[]{:S(2)}) async-start(), calls=%async_computation.3 | async-start | bytes 8388608 | tf_op jit(solution)/shard_map/psum | solution.py:24
  903.2 1.5 copy-start.3
  1054.6 613.1 %all-reduce.15.cloned.1.call-start = ((), (), s32[]{:S(2)}) async-start(), calls=%async_computation.4 | async-start | bytes 2097152 | tf_op jit(solution)/shard_map/psum | solution.py:79
  1142.6 93.0 %collective-permute-start.5 = (f32[2,512,512]{2,1,0:T(8,128)S(1)}, f32[2,512,512]{2,1,0:T(8,128)S(1)}, u32[]{:S(2)}, u32[]{:S(2)}) collective-permute-start(f32[2,512,512]{2,1,0:T(8,128)S(1)} %bitcast.193), channel_id=1, source_target_pairs={{0,16},{16,0},{4,20},{20,4},{8,24},{24,8},{12,28},{28,12},{1,17},{... | collective-permute-start | bytes 6291464 | tf_op jit(solution)/shard_map/ppermute | solution.py:34
  1236.3 24.2 %collective-permute-start.6 = (f32[1,512,512]{2,1,0:T(8,128)S(1)}, f32[1,512,512]{2,1,0:T(8,128)S(1)}, u32[]{:S(2)}, u32[]{:S(2)}) collective-permute-start(f32[1,512,512]{2,1,0:T(8,128)S(1)} %slice_select_fusion.4), channel_id=1, source_target_pairs={{0,8},{8,0},{4,12},{12,4},{16,24},{24,16},{20,28},{28,20},{1,9},{9... | collective-permute-start | bytes 3145736 | tf_op jit(solution)/shard_map/ppermute | solution.py:34
  1260.9 23.4 %collective-permute-start.7 = (f32[512,512]{1,0:T(8,128)S(1)}, f32[512,512]{1,0:T(8,128)S(1)}, u32[]{:S(2)}, u32[]{:S(2)}) collective-permute-start(f32[512,512]{1,0:T(8,128)S(1)} %select_bitcast_fusion.1), channel_id=1, source_target_pairs={{0,4},{4,0},{8,12},{12,8},{16,20},{20,16},{24,28},{28,24},{1,5},{5... | collective-permute-start | bytes 3145736 | tf_op jit(solution)/shard_map/ppermute | solution.py:14
  1284.5 53.3 %copy-start.5 = (f32[512,512]{1,0:T(8,128)S(1)}, f32[512,512]{1,0:T(8,128)}, u32[]{:S(2)}) copy-start(f32[512,512]{1,0:T(8,128)} %get-tuple-element.169) | copy-start | bytes 3145732
  1284.5 46.5 %collective-permute-start.8 = (f32[1024,512]{1,0:T(8,128)S(1)}, f32[1024,512]{1,0:T(8,128)S(1)}, u32[]{:S(2)}, u32[]{:S(2)}) collective-permute-start(f32[1024,512]{1,0:T(8,128)S(1)} %maximum_select_fusion.5), channel_id=1, source_target_pairs={{0,8},{4,12},{8,0},{12,4},{16,24},{20,28},{24,16},{28,20},{1,9},{5... | collective-permute-start | bytes 6291464 | tf_op jit(solution)/shard_map/ppermute | solution.py:14
  1333.8 182.6 %collective-permute-start.9 = (f32[2048,512]{1,0:T(8,128)}, f32[2048,512]{1,0:T(8,128)}, u32[]{:S(2)}, u32[]{:S(2)}) collective-permute-start(f32[2048,512]{1,0:T(8,128)} %maximum_select_fusion.3), channel_id=1, source_target_pairs={{0,16},{4,20},{8,24},{12,28},{16,0},{20,4},{24,8},{28,12},{1,17},{... | collective-permute-start | bytes 12582920 | tf_op jit(solution)/shard_map/ppermute | solution.py:14
  1522.8 2.2 copy-start.1
  1667.7 1.5 copy-start.4
  1808.3 8.7 copy-start.6
Sparse Core Ops, SparseCore 0:
  32.7 81.0 all-reduce.6
  275.7 84.1 all-reduce.8
  825.0 78.1 all-reduce.10
  1054.7 85.0 all-reduce.12
  1589.2 78.4 all-reduce.14
